TPU v7x, 512 devices: a whole 4x4x16 slice. The times are simulated.
512 devices in a mesh: dp: 32 (over y_hi, z), tensor: 16 (over x, y_lo, core).
Axes of the slice: x: 4, y: 4 (y_hi: 2, y_lo: 2; y = y_hi * 2 + y_lo), z: 16, core: 2. Of those that a mesh axis runs over, the one named last changes fastest.
Arguments:
- residual: bfloat16 [65536, 2048], P(('dp', 'tensor')), may hold values from -0.59765625 to 0.59765625
- queries: bfloat16 [65536, 2048], P(('dp', 'tensor')), may hold values from -27 to 27
- new_keys: bfloat16 [65536, 2048], P(('dp', 'tensor')), may hold values from -27 to 27
- new_values: bfloat16 [65536, 2048], P(('dp', 'tensor')), may hold values from -6 to 6
- lengths: int32 [32, 2], P('dp'), may hold values from 1 to 1536, 2048 in all within a row
- page_order: int32 [32, 17], P('dp'), may hold values from 0 to 16, each once within a row
- wo_shard: float32 [2048, 2048], P('tensor', 'dp'), may hold values from -0.125 to 0.125
- norm_gain: float32 [2048], replicated, may hold values from 0.1 to 1.9
- gate_shard: float32 [16, 2048, 256], P('tensor', 'dp'), may hold values from -0.125 to 0.125
- up_shard: float32 [16, 2048, 256], P('tensor', 'dp'), may hold values from -0.125 to 0.125
- down_shard: float32 [16, 256, 2048], P('tensor', None, 'dp'), may hold values from -0.1875 to 0.1875
- routes: int32 [65536, 8], P(('dp', 'tensor')), may hold values from 0 to 63, as said below
- route_weights: float32 [65536, 8], P(('dp', 'tensor')), may hold values from 0.05 to 0.3
Outputs:
- hidden_mid: bfloat16 [65536, 2048], P(('dp', 'tensor'))
- expert_sum: bfloat16 [65536, 2048], P(('dp', 'tensor'))
- key_pages: bfloat16 [544, 128, 2048], P('dp', None, 'tensor')
- value_pages: bfloat16 [544, 128, 2048], P('dp', None, 'tensor')
Inputs may be any that keep to these rules, and one draw needn't show every extreme that they name: `routes`: each row names 8 different experts. Within each aligned block of 128 rows (the rows of one device), each expert below 4 is named by 1 to 16 rows; one of them, the same in all blocks of a draw, by exactly 16 rows in every block, the others by at most 8 rows.
All inputs are finite; a program needn't handle non-finite values.
Results may differ from a plain program's by a relative error of at most 0.015.
Values may be sent and summed in bfloat16 or wider, within the bound.
No kernel may reach another device: no remote copies, remote signals or barrier semaphores. Data moves between devices by JAX's collectives and lax.ppermute only.
A program may use at most 64 MiB of HBM per device.

v0:
```python
import math
import jax
import jax.numpy as jnp
from jax import lax
from jax.sharding import Mesh, PartitionSpec as P

D = 2048
HEADS = 16
HD = 128
SPLIT = 4
PAGE = 128
MOST = 16


def page_layout(lens_row, order_row, group_rows, pool_size):
    index_rows = jnp.arange(group_rows, dtype=jnp.int32)
    prompt_ends = jnp.cumsum(lens_row)
    segment = jnp.sum((index_rows[:, None] >= prompt_ends[None, :]).astype(jnp.int32), axis=1)
    prompt_starts = prompt_ends - lens_row
    owner_mask = (
        segment[:, None] == jnp.arange(lens_row.shape[0], dtype=jnp.int32)[None, :]
    ).astype(jnp.int32)
    begins = jnp.sum(owner_mask * prompt_starts[None, :], axis=1)
    page_count = (lens_row + PAGE - 1) // PAGE
    first_page = jnp.cumsum(page_count) - page_count
    page_first = jnp.sum(owner_mask * first_page[None, :], axis=1)
    position = index_rows - begins
    logical = page_first + position // PAGE
    matched = (logical[:, None] == jnp.arange(pool_size, dtype=jnp.int32)[None, :]).astype(
        jnp.int32
    )
    physical = jnp.sum(matched * order_row[None, :], axis=1)
    return (segment, physical * PAGE + position % PAGE)


def attend_group(q_heads, k_heads, v_heads, segment, heads_here):
    group_rows = q_heads.shape[0]
    block_rows = min(512, group_rows)
    count_blocks = group_rows // block_rows
    q_blocks = q_heads.reshape(count_blocks, block_rows, heads_here, HD)
    seg_blocks = segment.reshape(count_blocks, block_rows)
    k_split = k_heads.reshape(group_rows, heads_here, HD)
    v_split = v_heads.reshape(group_rows, heads_here, HD)

    def one_block(block_pair):
        q_block, seg_block = block_pair
        scores = jnp.einsum(
            "qhd,khd->hqk", q_block, k_split, preferred_element_type=jnp.float32
        ) / math.sqrt(HD)
        same_prompt = seg_block[:, None] == segment[None, :]
        scores = jnp.where(same_prompt[None, :, :], scores, -jnp.inf)
        row_max = jnp.max(scores, axis=2, keepdims=True)
        weights = jnp.exp(scores - row_max)
        totals = jnp.sum(weights, axis=2)
        output = jnp.einsum(
            "hqk,khd->qhd",
            weights.astype(jnp.bfloat16),
            v_split,
            preferred_element_type=jnp.float32,
        )
        output = output / jnp.transpose(totals)[:, :, None]
        return output.astype(jnp.bfloat16).reshape(block_rows, heads_here * HD)

    return lax.map(one_block, (q_blocks, seg_blocks)).reshape(group_rows, heads_here * HD)


def body(
    residual,
    queries,
    new_keys,
    new_values,
    lengths,
    page_order,
    wo_shard,
    norm_gain,
    gate_shard,
    up_shard,
    down_shard,
    routes,
    route_weights,
):
    tensor_count = lax.axis_size("tensor")
    heads_here = HEADS // tensor_count
    q_heads, k_heads, v_heads = (
        lax.all_to_all(queries, "tensor", split_axis=1, concat_axis=0, tiled=True),
        lax.all_to_all(new_keys, "tensor", split_axis=1, concat_axis=0, tiled=True),
        lax.all_to_all(new_values, "tensor", split_axis=1, concat_axis=0, tiled=True),
    )
    group_rows = q_heads.shape[0]
    pool_size = page_order.shape[1]
    segment, slot_index = page_layout(lengths[0], page_order[0], group_rows, pool_size)
    head_width = k_heads.shape[1]
    key_pages = (
        jnp.zeros((pool_size * PAGE, head_width), jnp.bfloat16)
        .at[slot_index]
        .set(k_heads)
        .reshape(pool_size, PAGE, head_width)
    )
    value_pages = (
        jnp.zeros((pool_size * PAGE, head_width), jnp.bfloat16)
        .at[slot_index]
        .set(v_heads)
        .reshape(pool_size, PAGE, head_width)
    )
    pieces = [
        wo_shard.astype(jnp.bfloat16).T,
        gate_shard[0].astype(jnp.bfloat16),
        up_shard[0].astype(jnp.bfloat16),
        down_shard[0].astype(jnp.bfloat16),
    ]
    packed = jnp.concatenate([p.reshape(-1) for p in pieces]).reshape(-1, 128)
    gathered = lax.all_gather(lax.all_gather(packed, "dh"), "dz")
    gathered, q_heads, k_heads, v_heads, key_pages, value_pages = lax.optimization_barrier(
        (gathered, q_heads, k_heads, v_heads, key_pages, value_pages)
    )
    wo_piece_rows = pieces[0].size // 128
    wo_cols = jnp.swapaxes(gathered[:, :, :wo_piece_rows], 0, 1).reshape(-1, pieces[0].shape[1])
    wo_full = lax.all_gather(wo_cols, "tensor", axis=1, tiled=True)
    experts = jnp.swapaxes(gathered[:, :, wo_piece_rows:], 0, 1)
    experts = experts.reshape(experts.shape[0] * experts.shape[1], -1)
    weights_full, at = ([], 0)
    for p in pieces[1:]:
        weights_full.append(experts[:, at : at + p.size].reshape((-1,) + p.shape))
        at += p.size
    gate_full = weights_full[0].reshape(1, -1, gate_shard.shape[2])
    up_full = weights_full[1].reshape(1, -1, up_shard.shape[2])
    down_full = weights_full[2].transpose(1, 0, 2).reshape(1, down_shard.shape[1], -1)
    attended = attend_group(q_heads, k_heads, v_heads, segment, heads_here)
    token_rows = lax.all_to_all(attended, "tensor", split_axis=0, concat_axis=1, tiled=True)
    projected = jnp.einsum("tr,cr->tc", token_rows, wo_full, preferred_element_type=jnp.float32)
    hidden_mid = (residual.astype(jnp.float32) + projected).astype(jnp.bfloat16)
    mid_float = hidden_mid.astype(jnp.float32)
    normed = (
        mid_float
        * lax.rsqrt(jnp.mean(mid_float * mid_float, axis=1, keepdims=True) + 1e-06)
        * norm_gain
    ).astype(jnp.bfloat16)
    flight = tensor_count // SPLIT
    flight_ids = jnp.arange(flight, dtype=jnp.int32)
    named_here = routes[:, :, None] == flight_ids[None, None, :]
    routed = jnp.any(named_here, axis=1)
    weight_sum = jnp.sum(jnp.where(named_here, route_weights[:, :, None], 0.0), axis=1)
    ranked = jnp.cumsum(routed.astype(jnp.int32), axis=0) - 1
    picked = (ranked[:, :, None] == jnp.arange(MOST, dtype=jnp.int32)[None, None, :]) & routed[
        :, :, None
    ]
    outgoing = jnp.einsum(
        "tem,td->emd", picked.astype(jnp.bfloat16), normed, preferred_element_type=jnp.float32
    ).astype(jnp.bfloat16)
    outgoing = jnp.repeat(outgoing, SPLIT, axis=0)
    arrived = lax.all_to_all(outgoing, "tensor", split_axis=0, concat_axis=0, tiled=True)
    gate_val = jnp.einsum("smd,dp->smp", arrived, gate_full[0], preferred_element_type=jnp.float32)
    up_val = jnp.einsum("smd,dp->smp", arrived, up_full[0], preferred_element_type=jnp.float32)
    inner_act = (jax.nn.silu(gate_val) * up_val).astype(jnp.bfloat16)
    result = jnp.einsum(
        "smp,pd->smd", inner_act, down_full[0], preferred_element_type=jnp.float32
    ).astype(jnp.bfloat16)
    returned = lax.all_to_all(result, "tensor", split_axis=0, concat_axis=0, tiled=True)
    summed = jnp.sum(returned.reshape(flight, SPLIT, MOST, D).astype(jnp.float32), axis=1)
    mixing = picked.astype(jnp.float32) * weight_sum[:, :, None]
    expert_sum = jnp.einsum("tem,emd->td", mixing, summed, precision=lax.Precision.HIGHEST).astype(
        jnp.bfloat16
    )
    return (hidden_mid, expert_sum, key_pages, value_pages)


def solution(mesh):
    dp_count = mesh.shape["dp"]
    dz_count = 16 if dp_count % 16 == 0 else dp_count
    split_mesh = Mesh(
        mesh.devices.reshape(dp_count // dz_count, dz_count, mesh.shape["tensor"]),
        ("dh", "dz", "tensor"),
    )
    return jax.shard_map(
        body,
        mesh=split_mesh,
        in_specs=(
            P(("dh", "dz", "tensor"), None),
            P(("dh", "dz", "tensor"), None),
            P(("dh", "dz", "tensor"), None),
            P(("dh", "dz", "tensor"), None),
            P(("dh", "dz"), None),
            P(("dh", "dz"), None),
            P("tensor", ("dh", "dz")),
            P(),
            P("tensor", ("dh", "dz"), None),
            P("tensor", ("dh", "dz"), None),
            P("tensor", None, ("dh", "dz")),
            P(("dh", "dz", "tensor"), None),
            P(("dh", "dz", "tensor"), None),
        ),
        out_specs=(
            P(("dh", "dz", "tensor"), None),
            P(("dh", "dz", "tensor"), None),
            P(("dh", "dz"), None, "tensor"),
            P(("dh", "dz"), None, "tensor"),
        ),
        check_vma=False,
    )
```

profile of v0, /device:TPU:224, one launch (start us, length us, event | category | flops | bytes accessed | tf_op | source)
XLA Modules:
  0.0 236.6 jit_solution(14341236253968236352)
XLA Ops:
  7.2 0.8 convert_bitcast_fusion.2
  8.1 0.8 convert_bitcast_fusion.1
  9.0 0.8 convert_bitcast_fusion
  9.8 0.8 convert_element_type.85
  10.9 7.2 %all_gather.12 = bf16[2,448,128]{2,1,0:T(8,128)(2,1)} all-gather(bf16[1,448,128]{2,1,0:T(8,128)(2,1)S(1)} %maximum_bitcast_fusion), channel_id=1, replica_groups=mesh['dh'=2,'dz'=16,'tensor'=16] {'dh'}, dimensions={0}, use_global_device_ids=true | all-gather | bytes 344064 | tf_op jit(solution)/shard_map/all_gather | solution.py:112
  18.1 0.9 copy_bitcast_fusion.2
  19.1 5.4 %all-to-all-start.1 = ((bf16[128,16,128]{2,0,1:T(8,128)(2,1)}), bf16[128,16,128]{2,0,1:T(8,128)(2,1)S(1)}, u32[]{:S(2)}, u32[]{:S(2)}) async-start(bf16[128,16,128]{2,0,1:T(8,128)(2,1)} %copy_bitcast_fusion.2), calls=%async_computation.1 | async-start | bytes 1048576 | tf_op jit(solution)/shard_map/all_to_all | solution.py:86
  24.5 0.8 reduce-window.6
  26.4 2.0 copy_bitcast_fusion.1
  28.4 7.0 %all-to-all-done.1 = bf16[128,16,128]{2,0,1:T(8,128)(2,1)S(1)} async-done(((bf16[128,16,128]{2,0,1:T(8,128)(2,1)}), bf16[128,16,128]{2,0,1:T(8,128)(2,1)S(1)}, u32[]{:S(2)}, u32[]{:S(2)}) %all-to-all-start.1) | async-done | bytes 524320 | tf_op jit(solution)/shard_map/all_to_all | solution.py:86
  35.3 3.6 %all-to-all-start.2 = ((bf16[128,16,128]{2,0,1:T(8,128)(2,1)}), bf16[128,16,128]{2,0,1:T(8,128)(2,1)S(1)}, u32[]{:S(2)}, u32[]{:S(2)}) async-start(bf16[128,16,128]{2,0,1:T(8,128)(2,1)} %copy_bitcast_fusion.1), calls=%async_computation.2 | async-start | bytes 1048576 | tf_op jit(solution)/shard_map/all_to_all | solution.py:87
  39.0 0.9 copy_bitcast_fusion.3
  40.0 9.7 %all-to-all-done.2 = bf16[128,16,128]{2,0,1:T(8,128)(2,1)S(1)} async-done(((bf16[128,16,128]{2,0,1:T(8,128)(2,1)}), bf16[128,16,128]{2,0,1:T(8,128)(2,1)S(1)}, u32[]{:S(2)}, u32[]{:S(2)}) %all-to-all-start.2) | async-done | bytes 524320 | tf_op jit(solution)/shard_map/all_to_all | solution.py:87
  49.7 3.6 %all-to-all-start = ((bf16[128,16,128]{2,0,1:T(8,128)(2,1)}), bf16[128,16,128]{2,0,1:T(8,128)(2,1)S(1)}, u32[]{:S(2)}, u32[]{:S(2)}) async-start(bf16[128,16,128]{2,0,1:T(8,128)(2,1)} %copy_bitcast_fusion.3), calls=%async_computation | async-start | bytes 1048576 | tf_op jit(solution)/shard_map/all_to_all | solution.py:85
  53.4 6.5 %scatter_custom_fusion.1 = bf16[2176,128]{1,0:T(8,128)(2,1)} fusion(s32[2048]{0:T(1024)S(1)} %bitcast.161, bf16[2048,128]{1,0:T(8,128)(2,1)S(1)} %bitcast.140, bf16[]{:T(256)} %constant.81.clone.1), kind=kCustom, calls=%fused_computation.42 | custom fusion | bytes 557058 | tf_op jit(solution)/shard_map/scatter | solution.py:102
  59.9 6.5 %scatter_custom_fusion = bf16[2176,128]{1,0:T(8,128)(2,1)} fusion(s32[2048]{0:T(1024)S(1)} %bitcast.162, bf16[2048,128]{1,0:T(8,128)(2,1)S(1)} %bitcast.153, bf16[]{:T(256)} %constant.81.clone.1), kind=kCustom, calls=%fused_computation.44 | custom fusion | bytes 557058 | tf_op jit(solution)/shard_map/scatter | solution.py:96
  66.5 27.6 %all-gather.6.cloned.1.call-done = bf16[32,448,128]{2,1,0:T(8,128)(2,1)} async-done(((bf16[2,448,128]{2,1,0:T(8,128)(2,1)}), bf16[32,448,128]{2,1,0:T(8,128)(2,1)}) %all-gather.6.cloned.1.call-update) | async-done | bytes 3670032 | tf_op jit(solution)/shard_map/all_gather | solution.py:112
  94.0 1.1 slice_bitcast_fusion.1
  95.1 0.8 copy.70
  96.3 12.2 %while.10 = (s32[]{:T(128)}, bf16[4,512,128]{2,1,0:T(8,128)(2,1)}, s32[4,512]{1,0:T(4,128)S(1)}, s32[2048]{0:T(1024)S(1)}, bf16[4,512,1,128]{3,1,2,0:T(8,128)(2,...) while((s32[]{:T(128)}, bf16[4,512,128]{2,1,0:T(8,128)(2,1)}, ...), condition=%wide.region_11.12_spmd, body=%wide.region_8.11_spmd.sunk | while | flops 545389568 | bytes 13918313 | solution.py:64
  96.3 0.9 fusion.86
  97.2 0.7 fusion.87
  97.9 1.5 fusion.88
  99.4 0.9 fusion.86
  101.0 1.5 fusion.88
  102.4 0.9 fusion.86
  104.0 1.5 fusion.88
  105.5 0.9 fusion.86
  107.1 1.5 fusion.88
  108.5 5.3 %all-to-all-start.3 = ((bf16[16,128,128]{2,1,0:T(8,128)(2,1)}), bf16[16,128,128]{2,1,0:T(8,128)(2,1)S(1)}, u32[]{:S(2)}, u32[]{:S(2)}) async-start(bf16[16,128,128]{2,1,0:T(8,128)(2,1)} %bitcast.35), calls=%async_computation.3 | async-start | bytes 1048576 | tf_op jit(solution)/shard_map/all_to_all | solution.py:129
  113.9 2.3 slice_bitcast_fusion
  116.6 3.8 %copy.88 = bf16[4,8,384,128]{3,1,2,0:T(8,128)(2,1)} copy(bf16[4,8,384,128]{3,2,1,0:T(8,128)(2,1)S(1)} %bitcast.143) | data formatting | bytes 6291456
  120.4 7.0 %all-to-all-done.3 = bf16[16,128,128]{2,1,0:T(8,128)(2,1)S(1)} async-done(((bf16[16,128,128]{2,1,0:T(8,128)(2,1)}), bf16[16,128,128]{2,1,0:T(8,128)(2,1)S(1)}, u32[]{:S(2)}, u32[]{:S(2)}) %all-to-all-start.3) | async-done | bytes 524320 | tf_op jit(solution)/shard_map/all_to_all | solution.py:129
  127.6 43.4 %all-gather.4.cloned.1.call-done = bf16[2048,2048]{1,0:T(8,128)(2,1)} async-done(((bf16[2048,128]{1,0:T(8,128)(2,1)}), bf16[2048,2048]{1,0:T(8,128)(2,1)}) %all-gather.4.cloned.1.call-update) | async-done | bytes 8388624 | tf_op jit(solution)/shard_map/all_gather | solution.py:118
  171.1 6.4 %fusion.28 = (f32[128]{0:T(128)S(1)}, bf16[128,2048]{1,0:T(8,128)(2,1)S(1)}) fusion(bf16[128,2048]{0,1:T(8,128)(2,1)S(1)} %bitcast.147, bf16[2048,2048]{1,0:T(8,128)(2,1)} %all-gather.4.cloned.1.call-done, bf16[128,2048]{1,0:T(8,128)(2,1)S(1)} %copy-done.1), kind=kOutput, calls=%fused_computation.32 | convolution fusion | flops 1075314560 | bytes 9961984 | tf_op jit(solution)/shard_map/tr,cr->tc/dot_general | solution.py:130
  177.8 1.2 broadcast_in_dim.27
  179.0 6.1 %all-to-all-start.4 = ((bf16[16,16,2048]{2,1,0:T(8,128)(2,1)}), bf16[16,16,2048]{2,1,0:T(8,128)(2,1)}, u32[]{:S(2)}, u32[]{:S(2)}) async-start(bf16[16,16,2048]{2,1,0:T(8,128)(2,1)} %bitcast.41), calls=%async_computation.4 | async-start | bytes 2097152 | tf_op jit(solution)/shard_map/all_to_all | solution.py:151
  185.0 3.0 %fusion.66 = (bf16[32,16384]{1,0:T(8,128)(2,1)S(1)}, bf16[32,16384]{1,0:T(8,128)(2,1)}, bf16[32,16384]{1,0:T(8,128)(2,1)S(1)}) fusion(bf16[32,49152]{1,0:T(8,128)(2,1)} %bitcast.142), kind=kLoop, calls=%fused_computation.103 | loop fusion | bytes 6291456 | tf_op jit(solution)/shard_map/slice | solution.py:123
  188.1 1.3 reshape.276
  189.4 1.3 reshape.277
  190.7 3.0 %reshape.256 = bf16[32,256,64]{2,1,0:T(8,128)(2,1)S(1)} reshape(bf16[32,16384]{1,0:T(8,128)(2,1)} %get-tuple-element.101) | data formatting | bytes 2097152 | tf_op jit(solution)/shard_map/reshape | solution.py:123
  193.8 1.6 copy.74
  195.4 6.2 %all-to-all-done.4 = bf16[16,16,2048]{2,1,0:T(8,128)(2,1)} async-done(((bf16[16,16,2048]{2,1,0:T(8,128)(2,1)}), bf16[16,16,2048]{2,1,0:T(8,128)(2,1)}, u32[]{:S(2)}, u32[]{:S(2)}) %all-to-all-start.4) | async-done | bytes 1048608 | tf_op jit(solution)/shard_map/all_to_all | solution.py:151
  201.5 2.0 fusion.67
  203.5 4.2 %convolution_convert_fusion = bf16[16,16,2048]{2,1,0:T(8,128)(2,1)} fusion(bf16[256,2048,1]{0,1,2:T(8,128)(2,1)} %bitcast.150, bf16[16,16,2048]{2,1,0:T(8,128)(2,1)} %all-to-all-done.4, bf16[2048,256,1]{1,0,2:T(8,128)(2,1)} %reshape.277, f32[16,16,256]{2,1,0:T(8,128)S(1)} %fusion.67), kind=kOutput, calls=%fused_computation.21 | convolution fusion | flops 537788416 | bytes 4456448 | tf_op jit(solution)/shard_map/smp,pd->smd/dot_general | solution.py:155
  207.7 3.7 %all-to-all-start.5 = ((bf16[16,16,2048]{2,1,0:T(8,128)(2,1)}), bf16[16,16,2048]{2,1,0:T(8,128)(2,1)S(1)}, u32[]{:S(2)}, u32[]{:S(2)}) async-start(bf16[16,16,2048]{2,1,0:T(8,128)(2,1)} %convolution_convert_fusion), calls=%async_computation.5 | async-start | bytes 2097152 | tf_op jit(solution)/shard_map/all_to_all | solution.py:158
  211.4 16.4 %all-to-all-done.5 = bf16[16,16,2048]{2,1,0:T(8,128)(2,1)S(1)} async-done(((bf16[16,16,2048]{2,1,0:T(8,128)(2,1)}), bf16[16,16,2048]{2,1,0:T(8,128)(2,1)S(1)}, u32[]{:S(2)}, u32[]{:S(2)}) %all-to-all-start.5) | async-done | bytes 1048608 | tf_op jit(solution)/shard_map/all_to_all | solution.py:158
  227.9 1.8 fusion.26
  (56 shorter events, 5.3 us)
Async XLA Ops:
  7.2 11.0 %copy-start = (bf16[128,2048]{1,0:T(8,128)(2,1)S(1)}, bf16[128,2048]{1,0:T(8,128)(2,1)}, u32[]{:S(2)}) copy-start(bf16[128,2048]{1,0:T(8,128)(2,1)} %param.17) | copy-start | bytes 1572868
  7.2 31.7 %copy-start.6 = (s32[1,17]{1,0:T(1,128)S(1)}, s32[1,17]{1,0:T(1,128)}, u32[]{:S(2)}) copy-start(s32[1,17]{1,0:T(1,128)} %param.20) | copy-start | bytes 208
  7.2 31.8 %copy-start.3 = (bf16[128,2048]{1,0:T(8,128)(2,1)S(1)}, bf16[128,2048]{1,0:T(8,128)(2,1)}, u32[]{:S(2)}) copy-start(bf16[128,2048]{1,0:T(8,128)(2,1)} %param.16) | copy-start | bytes 1572868
  7.2 86.8 %all-gather.6.cloned.1.call-start = ((), (), s32[]{:S(2)}) async-start(), calls=%async_computation.7 | async-start | bytes 3899392 | tf_op jit(solution)/shard_map/all_gather | solution.py:112
  19.1 16.3 %all-to-all-start.1 = ((bf16[128,16,128]{2,0,1:T(8,128)(2,1)}), bf16[128,16,128]{2,0,1:T(8,128)(2,1)S(1)}, u32[]{:S(2)}, u32[]{:S(2)}) async-start(bf16[128,16,128]{2,0,1:T(8,128)(2,1)} %copy_bitcast_fusion.2), calls=%async_computation.1 | async-start | bytes 1048576 | tf_op jit(solution)/shard_map/all_to_all | solution.py:86
  24.5 71.5 %copy-start.4 = (s32[128,8]{0,1:T(8,128)S(1)}, s32[128,8]{0,1:T(8,128)}, u32[]{:S(2)}) copy-start(s32[128,8]{0,1:T(8,128)} %param.26) | copy-start | bytes 12292
  35.3 14.4 %all-to-all-start.2 = ((bf16[128,16,128]{2,0,1:T(8,128)(2,1)}), bf16[128,16,128]{2,0,1:T(8,128)(2,1)S(1)}, u32[]{:S(2)}, u32[]{:S(2)}) async-start(bf16[128,16,128]{2,0,1:T(8,128)(2,1)} %copy_bitcast_fusion.1), calls=%async_computation.2 | async-start | bytes 1048576 | tf_op jit(solution)/shard_map/all_to_all | solution.py:87
  49.7 16.8 %all-to-all-start = ((bf16[128,16,128]{2,0,1:T(8,128)(2,1)}), bf16[128,16,128]{2,0,1:T(8,128)(2,1)S(1)}, u32[]{:S(2)}, u32[]{:S(2)}) async-start(bf16[128,16,128]{2,0,1:T(8,128)(2,1)} %copy_bitcast_fusion.3), calls=%async_computation | async-start | bytes 1048576 | tf_op jit(solution)/shard_map/all_to_all | solution.py:85
  53.3 117.8 %all-gather.4.cloned.1.call-start = ((), (), s32[]{:S(2)}) async-start(), calls=%async_computation.6 | async-start | bytes 8912896 | tf_op jit(solution)/shard_map/all_gather | solution.py:118
  108.5 18.8 %all-to-all-start.3 = ((bf16[16,128,128]{2,1,0:T(8,128)(2,1)}), bf16[16,128,128]{2,1,0:T(8,128)(2,1)S(1)}, u32[]{:S(2)}, u32[]{:S(2)}) async-start(bf16[16,128,128]{2,1,0:T(8,128)(2,1)} %bitcast.35), calls=%async_computation.3 | async-start | bytes 1048576 | tf_op jit(solution)/shard_map/all_to_all | solution.py:129
  116.6 54.5 %copy-start.1 = (bf16[128,2048]{1,0:T(8,128)(2,1)S(1)}, bf16[128,2048]{1,0:T(8,128)(2,1)}, u32[]{:S(2)}) copy-start(bf16[128,2048]{1,0:T(8,128)(2,1)} %param.15) | copy-start | bytes 1572868
  171.1 6.4 %copy-start.7 = (f32[2048]{0:T(1024)S(1)}, f32[2048]{0:T(1024)}, u32[]{:S(2)}) copy-start(f32[2048]{0:T(1024)} %param.22) | copy-start | bytes 24580
  177.4 10.7 %copy-start.2 = (bf16[128,2048]{1,0:T(8,128)(2,1)}, bf16[128,2048]{1,0:T(8,128)(2,1)S(1)}, u32[]{:S(2)}) copy-start(bf16[128,2048]{1,0:T(8,128)(2,1)S(1)} %get-tuple-element.106) | copy-start | bytes 1572868
  179.0 22.6 %all-to-all-start.4 = ((bf16[16,16,2048]{2,1,0:T(8,128)(2,1)}), bf16[16,16,2048]{2,1,0:T(8,128)(2,1)}, u32[]{:S(2)}, u32[]{:S(2)}) async-start(bf16[16,16,2048]{2,1,0:T(8,128)(2,1)} %bitcast.41), calls=%async_computation.4 | async-start | bytes 2097152 | tf_op jit(solution)/shard_map/all_to_all | solution.py:151
  195.4 16.0 %copy-start.5 = (f32[128,8]{0,1:T(8,128)S(1)}, f32[128,8]{0,1:T(8,128)}, u32[]{:S(2)}) copy-start(f32[128,8]{0,1:T(8,128)} %param.27) | copy-start | bytes 12292
  207.7 20.1 %all-to-all-start.5 = ((bf16[16,16,2048]{2,1,0:T(8,128)(2,1)}), bf16[16,16,2048]{2,1,0:T(8,128)(2,1)S(1)}, u32[]{:S(2)}, u32[]{:S(2)}) async-start(bf16[16,16,2048]{2,1,0:T(8,128)(2,1)} %convolution_convert_fusion), calls=%async_computation.5 | async-start | bytes 2097152 | tf_op jit(solution)/shard_map/all_to_all | solution.py:158
Sparse Core Ops, SparseCore 0:
  18.2 75.7 all-gather.5
  96.7 74.3 all-gather.3
where the time goes:
time: 238 us; the launch traced here: 237 us
  waiting for transfers between devices  117 us (49%)
  local copies, waits for them, and re-layouts  37.5 us (16%)
  starting transfers between devices  27.6 us (12%)
  matrix products  24 us (10%)
  between operations  14.3 us (6%)
  other arithmetic  8.66 us (4%)
  blocking collectives  7.16 us (3%)
    all_gather x1, waiting for transfers between devices, body(): wo_full = lax.all_gather(wo_cols, 'tensor', axis=1, tiled=True)  43.4 us
    all_gather x1, waiting for transfers between devices, body(): gathered = lax.all_gather(lax.all_gather(packed, 'dh'), 'dz')  27.6 us
    all_to_all x1, waiting for transfers between devices, body(): lax.all_to_all(result, 'tensor', split_axis=0, concat_axis=0, tiled=True)  16.4 us
    all_to_all x1, waiting for transfers between devices, body(): lax.all_to_all(new_values, 'tensor', split_axis=1, concat_axis=0, tiled=T...  9.71 us
    all_gather x1, blocking collectives, body(): gathered = lax.all_gather(lax.all_gather(packed, 'dh'), 'dz')  7.16 us
    all_to_all x1, waiting for transfers between devices, body(): lax.all_to_all(attended, 'tensor', split_axis=0, concat_axis=1, tiled=True)  7 us
    all_to_all x1, waiting for transfers between devices, body(): lax.all_to_all(new_keys, 'tensor', split_axis=1, concat_axis=0, tiled=True)  6.95 us
    scatter x1, local copies, waits for them, and re-layouts, body(): value_pages = jnp.zeros((pool_size * PAGE, head_width), jnp.bfloat16).at[...  6.54 us
  transfers between devices with their start and end apart: 8, of which 7 were waited for; matrix products, arithmetic and copies ran while one was open for 21% of the time, Pallas kernels for 0%

commit v1 on v0

--- a/solution.py
+++ b/solution.py
@@ -1,3 +1,4 @@
+import functools
 import math
 import jax
 import jax.numpy as jnp
@@ -10,6 +11,21 @@
 SPLIT = 4
 PAGE = 128
 MOST = 16
+
+
+def solve_packet_in(raw, named_axis, axis_no):
+    return jnp.concatenate(
+        jax.lax.all_to_all(
+            jnp.stack(tuple((raw for _ in range(jax.lax.axis_size(named_axis)))), axis=0),
+            axis_name=named_axis,
+            concat_axis=0,
+            split_axis=0,
+        ),
+        axis=axis_no,
+    )
+
+
+solve_the_strings = functools.partial(solve_packet_in, named_axis="tensor", axis_no=1)
 
 
 def page_layout(lens_row, order_row, group_rows, pool_size):
@@ -115,7 +131,7 @@
     )
     wo_piece_rows = pieces[0].size // 128
     wo_cols = jnp.swapaxes(gathered[:, :, :wo_piece_rows], 0, 1).reshape(-1, pieces[0].shape[1])
-    wo_full = lax.all_gather(wo_cols, "tensor", axis=1, tiled=True)
+    wo_full = solve_the_strings(wo_cols)
     experts = jnp.swapaxes(gathered[:, :, wo_piece_rows:], 0, 1)
     experts = experts.reshape(experts.shape[0] * experts.shape[1], -1)
     weights_full, at = ([], 0)

time: 238 us -> 338 us (1.42)
  the two profiles are of different devices: /device:TPU:224 before, /device:TPU:1 now
where the time goes in v1:
time: 338 us; the launch traced here: 336 us
  waiting for transfers between devices  186 us (55%)
  starting transfers between devices  55.3 us (16%)
  local copies, waits for them, and re-layouts  41.9 us (12%)
  matrix products  23.9 us (7%)
  between operations  14.2 us (4%)
  other arithmetic  8.65 us (3%)
  blocking collectives  6.67 us (2%)
    all_to_all x1, waiting for transfers between devices, solve_packet_in(): jax.lax.all_to_all(jnp.stack(tuple((raw for _ in range(jax.lax.axis_size(...  121 us
    all_gather x1, waiting for transfers between devices, body(): gathered = lax.all_gather(lax.all_gather(packed, 'dh'), 'dz')  20.5 us
    all_to_all x1, waiting for transfers between devices, body(): lax.all_to_all(result, 'tensor', split_axis=0, concat_axis=0, tiled=True)  15.5 us
    all_to_all x1, starting transfers between devices, body(): lax.all_to_all(attended, 'tensor', split_axis=0, concat_axis=1, tiled=True)  14.8 us
    all_to_all x1, starting transfers between devices, body(): lax.all_to_all(new_keys, 'tensor', split_axis=1, concat_axis=0, tiled=True)  10.6 us
    all_to_all x1, starting transfers between devices, body(): lax.all_to_all(outgoing, 'tensor', split_axis=0, concat_axis=0, tiled=True)  10.2 us
    all_to_all x1, waiting for transfers between devices, body(): lax.all_to_all(new_values, 'tensor', split_axis=1, concat_axis=0, tiled=T...  8.68 us
    all_to_all x1, waiting for transfers between devices, body(): lax.all_to_all(attended, 'tensor', split_axis=0, concat_axis=1, tiled=True)  8.57 us
  transfers between devices with their start and end apart: 8, of which 7 were waited for; matrix products, arithmetic and copies ran while one was open for 11% of the time, Pallas kernels for 0%

profile of v1, /device:TPU:1, one launch (start us, length us, event | category | flops | bytes accessed | tf_op | source)
XLA Modules:
  0.0 336.5 jit_solution(10735120357280760331)
XLA Ops:
  7.2 0.8 convert_bitcast_fusion.2
  8.1 0.8 convert_bitcast_fusion.1
  9.0 0.8 convert_bitcast_fusion
  9.8 0.8 convert_element_type.85
  10.9 6.7 %all_gather.9 = bf16[2,448,128]{2,1,0:T(8,128)(2,1)} all-gather(bf16[1,448,128]{2,1,0:T(8,128)(2,1)S(1)} %maximum_bitcast_fusion), channel_id=1, replica_groups=mesh['dh'=2,'dz'=16,'tensor'=16] {'dh'}, dimensions={0}, use_global_device_ids=true | all-gather | bytes 344064 | tf_op jit(solution)/shard_map/all_gather | solution.py:128
  17.6 0.9 copy_bitcast_fusion.2
  18.6 10.6 %all-to-all-start.1 = ((bf16[128,16,128]{2,0,1:T(8,128)(2,1)}), bf16[128,16,128]{2,0,1:T(8,128)(2,1)S(1)}, u32[]{:S(2)}, u32[]{:S(2)}) async-start(bf16[128,16,128]{2,0,1:T(8,128)(2,1)} %copy_bitcast_fusion.2), calls=%async_computation.1 | async-start | bytes 1048576 | tf_op jit(solution)/shard_map/all_to_all | solution.py:102
  29.2 0.8 reduce-window.6
  31.0 2.0 copy_bitcast_fusion.1
  33.0 5.9 %all-to-all-done.1 = bf16[128,16,128]{2,0,1:T(8,128)(2,1)S(1)} async-done(((bf16[128,16,128]{2,0,1:T(8,128)(2,1)}), bf16[128,16,128]{2,0,1:T(8,128)(2,1)S(1)}, u32[]{:S(2)}, u32[]{:S(2)}) %all-to-all-start.1) | async-done | bytes 524320 | tf_op jit(solution)/shard_map/all_to_all | solution.py:102
  38.9 4.6 %all-to-all-start.2 = ((bf16[128,16,128]{2,0,1:T(8,128)(2,1)}), bf16[128,16,128]{2,0,1:T(8,128)(2,1)S(1)}, u32[]{:S(2)}, u32[]{:S(2)}) async-start(bf16[128,16,128]{2,0,1:T(8,128)(2,1)} %copy_bitcast_fusion.1), calls=%async_computation.2 | async-start | bytes 1048576 | tf_op jit(solution)/shard_map/all_to_all | solution.py:103
  43.7 0.9 copy_bitcast_fusion.3
  44.6 8.7 %all-to-all-done.2 = bf16[128,16,128]{2,0,1:T(8,128)(2,1)S(1)} async-done(((bf16[128,16,128]{2,0,1:T(8,128)(2,1)}), bf16[128,16,128]{2,0,1:T(8,128)(2,1)S(1)}, u32[]{:S(2)}, u32[]{:S(2)}) %all-to-all-start.2) | async-done | bytes 524320 | tf_op jit(solution)/shard_map/all_to_all | solution.py:103
  53.3 4.6 %all-to-all-start = ((bf16[128,16,128]{2,0,1:T(8,128)(2,1)}), bf16[128,16,128]{2,0,1:T(8,128)(2,1)S(1)}, u32[]{:S(2)}, u32[]{:S(2)}) async-start(bf16[128,16,128]{2,0,1:T(8,128)(2,1)} %copy_bitcast_fusion.3), calls=%async_computation | async-start | bytes 1048576 | tf_op jit(solution)/shard_map/all_to_all | solution.py:101
  58.0 6.5 %scatter_custom_fusion.1 = bf16[2176,128]{1,0:T(8,128)(2,1)} fusion(s32[2048]{0:T(1024)S(1)} %bitcast.177, bf16[2048,128]{1,0:T(8,128)(2,1)S(1)} %bitcast.158, bf16[]{:T(256)} %constant.81.clone.1), kind=kCustom, calls=%fused_computation.46 | custom fusion | bytes 557058 | tf_op jit(solution)/shard_map/scatter | solution.py:118
  64.5 6.5 %scatter_custom_fusion = bf16[2176,128]{1,0:T(8,128)(2,1)} fusion(s32[2048]{0:T(1024)S(1)} %bitcast.178, bf16[2048,128]{1,0:T(8,128)(2,1)S(1)} %bitcast.169, bf16[]{:T(256)} %constant.81.clone.1), kind=kCustom, calls=%fused_computation.48 | custom fusion | bytes 557058 | tf_op jit(solution)/shard_map/scatter | solution.py:112
  71.1 20.5 %all-gather.3.cloned.1.call-done = bf16[32,448,128]{2,1,0:T(8,128)(2,1)} async-done(((bf16[2,448,128]{2,1,0:T(8,128)(2,1)}), bf16[32,448,128]{2,1,0:T(8,128)(2,1)}) %all-gather.3.cloned.1.call-update) | async-done | bytes 3670032 | tf_op jit(solution)/shard_map/all_gather | solution.py:128
  91.6 12.2 %while.10 = (s32[]{:T(128)}, bf16[4,512,128]{2,1,0:T(8,128)(2,1)}, s32[4,512]{1,0:T(4,128)S(1)}, s32[2048]{0:T(1024)S(1)}, bf16[4,512,1,128]{3,1,2,0:T(8,128)(2,...) while((s32[]{:T(128)}, bf16[4,512,128]{2,1,0:T(8,128)(2,1)}, ...), condition=%wide.region_11.12_spmd, body=%wide.region_8.11_spmd.sunk | while | flops 545389568 | bytes 13918313 | solution.py:80
  91.6 0.9 fusion.95
  93.2 1.5 fusion.97
  94.6 0.9 fusion.95
  96.2 1.5 fusion.97
  97.7 0.9 fusion.95
  99.3 1.5 fusion.97
  100.7 0.9 fusion.95
  102.3 1.5 fusion.97
  103.8 14.8 %all-to-all-start.3 = ((bf16[16,128,128]{2,1,0:T(8,128)(2,1)}), bf16[16,128,128]{2,1,0:T(8,128)(2,1)S(1)}, u32[]{:S(2)}, u32[]{:S(2)}) async-start(bf16[16,128,128]{2,1,0:T(8,128)(2,1)} %bitcast.35), calls=%async_computation.3 | async-start | bytes 1048576 | tf_op jit(solution)/shard_map/all_to_all | solution.py:145
  118.6 1.1 slice_bitcast_fusion.1
  119.7 8.6 %all-to-all-done.3 = bf16[16,128,128]{2,1,0:T(8,128)(2,1)S(1)} async-done(((bf16[16,128,128]{2,1,0:T(8,128)(2,1)}), bf16[16,128,128]{2,1,0:T(8,128)(2,1)S(1)}, u32[]{:S(2)}, u32[]{:S(2)}) %all-to-all-start.3) | async-done | bytes 524320 | tf_op jit(solution)/shard_map/all_to_all | solution.py:145
  128.3 4.8 %stack.3 = bf16[16,2048,128]{2,1,0:T(8,128)(2,1)} broadcast(bf16[2048,128]{1,0:T(8,128)(2,1)S(1)} %bitcast.165), dimensions={1,2} | broadcast | bytes 8912896 | tf_op jit(solution)/shard_map/stack | solution.py:19
  133.1 5.8 %all-to-all-start.4 = ((bf16[16,2048,128]{2,1,0:T(8,128)(2,1)}), bf16[16,2048,128]{2,1,0:T(8,128)(2,1)}, u32[]{:S(2)}, u32[]{:S(2)}) async-start(bf16[16,2048,128]{2,1,0:T(8,128)(2,1)} %stack.3), calls=%async_computation.4 | async-start | bytes 16777216 | tf_op jit(solution)/shard_map/all_to_all | solution.py:18
  139.3 2.2 slice_bitcast_fusion
  141.9 3.7 %copy.85 = bf16[4,8,384,128]{3,1,2,0:T(8,128)(2,1)} copy(bf16[4,8,384,128]{3,2,1,0:T(8,128)(2,1)S(1)} %bitcast.161) | data formatting | bytes 6291456
  145.6 121.4 %all-to-all-done.4 = bf16[16,2048,128]{2,1,0:T(8,128)(2,1)} async-done(((bf16[16,2048,128]{2,1,0:T(8,128)(2,1)}), bf16[16,2048,128]{2,1,0:T(8,128)(2,1)}, u32[]{:S(2)}, u32[]{:S(2)}) %all-to-all-start.4) | async-done | bytes 8388640 | tf_op jit(solution)/shard_map/all_to_all | solution.py:18
  267.0 6.3 %fusion.38 = (f32[128]{0:T(128)S(1)}, bf16[128,2048]{1,0:T(8,128)(2,1)S(1)}) fusion(bf16[16,2048,128]{2,1,0:T(8,128)(2,1)} %all-to-all-done.4, bf16[16,128,128]{2,1,0:T(8,128)(2,1)S(1)} %all-to-all-done.3, bf16[128,2048]{1,0:T(8,128)(2,1)S(1)} %copy-done.1), kind=kOutput, calls=%fused_computation.35 | convolution fusion | flops 1075314560 | bytes 9961984 | tf_op jit(solution)/shard_map/tr,cr->tc/dot_general | solution.py:146
  274.4 1.2 broadcast_in_dim.27
  275.6 10.2 %all-to-all-start.5 = ((bf16[16,16,2048]{2,1,0:T(8,128)(2,1)}), bf16[16,16,2048]{2,1,0:T(8,128)(2,1)}, u32[]{:S(2)}, u32[]{:S(2)}) async-start(bf16[16,16,2048]{2,1,0:T(8,128)(2,1)} %bitcast.42), calls=%async_computation.5 | async-start | bytes 2097152 | tf_op jit(solution)/shard_map/all_to_all | solution.py:167
  285.8 3.0 fusion.77
  288.8 1.3 reshape.280
  290.2 1.3 reshape.281
  291.5 3.0 reshape.259
  294.5 1.6 copy.71
  296.1 5.2 %all-to-all-done.5 = bf16[16,16,2048]{2,1,0:T(8,128)(2,1)} async-done(((bf16[16,16,2048]{2,1,0:T(8,128)(2,1)}), bf16[16,16,2048]{2,1,0:T(8,128)(2,1)}, u32[]{:S(2)}, u32[]{:S(2)}) %all-to-all-start.5) | async-done | bytes 1048608 | tf_op jit(solution)/shard_map/all_to_all | solution.py:167
  301.3 2.0 fusion.78
  303.3 4.2 %convolution_convert_fusion = bf16[16,16,2048]{2,1,0:T(8,128)(2,1)} fusion(bf16[256,2048,1]{0,1,2:T(8,128)(2,1)} %bitcast.166, bf16[16,16,2048]{2,1,0:T(8,128)(2,1)} %all-to-all-done.5, bf16[2048,256,1]{1,0,2:T(8,128)(2,1)} %reshape.281, f32[16,16,256]{2,1,0:T(8,128)S(1)} %fusion.78), kind=kOutput, calls=%fused_computation.23 | convolution fusion | flops 537788416 | bytes 4456448 | tf_op jit(solution)/shard_map/smp,pd->smd/dot_general | solution.py:171
  307.5 4.5 %all-to-all-start.6 = ((bf16[16,16,2048]{2,1,0:T(8,128)(2,1)}), bf16[16,16,2048]{2,1,0:T(8,128)(2,1)S(1)}, u32[]{:S(2)}, u32[]{:S(2)}) async-start(bf16[16,16,2048]{2,1,0:T(8,128)(2,1)} %convolution_convert_fusion), calls=%async_computation.6 | async-start | bytes 2097152 | tf_op jit(solution)/shard_map/all_to_all | solution.py:174
  312.1 15.5 %all-to-all-done.6 = bf16[16,16,2048]{2,1,0:T(8,128)(2,1)S(1)} async-done(((bf16[16,16,2048]{2,1,0:T(8,128)(2,1)}), bf16[16,16,2048]{2,1,0:T(8,128)(2,1)S(1)}, u32[]{:S(2)}, u32[]{:S(2)}) %all-to-all-start.6) | async-done | bytes 1048608 | tf_op jit(solution)/shard_map/all_to_all | solution.py:174
  327.8 1.8 fusion.36
  (55 shorter events, 6.5 us)
Async XLA Ops:
  7.2 10.5 %copy-start = (bf16[128,2048]{1,0:T(8,128)(2,1)S(1)}, bf16[128,2048]{1,0:T(8,128)(2,1)}, u32[]{:S(2)}) copy-start(bf16[128,2048]{1,0:T(8,128)(2,1)} %param.17) | copy-start | bytes 1572868
  7.2 36.4 %copy-start.6 = (s32[1,17]{1,0:T(1,128)S(1)}, s32[1,17]{1,0:T(1,128)}, u32[]{:S(2)}) copy-start(s32[1,17]{1,0:T(1,128)} %param.20) | copy-start | bytes 208
  7.2 36.5 %copy-start.3 = (bf16[128,2048]{1,0:T(8,128)(2,1)S(1)}, bf16[128,2048]{1,0:T(8,128)(2,1)}, u32[]{:S(2)}) copy-start(bf16[128,2048]{1,0:T(8,128)(2,1)} %param.16) | copy-start | bytes 1572868
  7.2 84.4 %all-gather.3.cloned.1.call-start = ((), (), s32[]{:S(2)}) async-start(), calls=%async_computation.7 | async-start | bytes 3899392 | tf_op jit(solution)/shard_map/all_gather | solution.py:128
  18.6 20.4 %all-to-all-start.1 = ((bf16[128,16,128]{2,0,1:T(8,128)(2,1)}), bf16[128,16,128]{2,0,1:T(8,128)(2,1)S(1)}, u32[]{:S(2)}, u32[]{:S(2)}) async-start(bf16[128,16,128]{2,0,1:T(8,128)(2,1)} %copy_bitcast_fusion.2), calls=%async_computation.1 | async-start | bytes 1048576 | tf_op jit(solution)/shard_map/all_to_all | solution.py:102
  38.9 14.4 %all-to-all-start.2 = ((bf16[128,16,128]{2,0,1:T(8,128)(2,1)}), bf16[128,16,128]{2,0,1:T(8,128)(2,1)S(1)}, u32[]{:S(2)}, u32[]{:S(2)}) async-start(bf16[128,16,128]{2,0,1:T(8,128)(2,1)} %copy_bitcast_fusion.1), calls=%async_computation.2 | async-start | bytes 1048576 | tf_op jit(solution)/shard_map/all_to_all | solution.py:103
  53.3 17.8 %all-to-all-start = ((bf16[128,16,128]{2,0,1:T(8,128)(2,1)}), bf16[128,16,128]{2,0,1:T(8,128)(2,1)S(1)}, u32[]{:S(2)}, u32[]{:S(2)}) async-start(bf16[128,16,128]{2,0,1:T(8,128)(2,1)} %copy_bitcast_fusion.3), calls=%async_computation | async-start | bytes 1048576 | tf_op jit(solution)/shard_map/all_to_all | solution.py:101
  103.8 24.5 %all-to-all-start.3 = ((bf16[16,128,128]{2,1,0:T(8,128)(2,1)}), bf16[16,128,128]{2,1,0:T(8,128)(2,1)S(1)}, u32[]{:S(2)}, u32[]{:S(2)}) async-start(bf16[16,128,128]{2,1,0:T(8,128)(2,1)} %bitcast.35), calls=%async_computation.3 | async-start | bytes 1048576 | tf_op jit(solution)/shard_map/all_to_all | solution.py:145
  133.1 5.8 %copy-start.4 = (s32[128,8]{0,1:T(8,128)S(1)}, s32[128,8]{0,1:T(8,128)}, u32[]{:S(2)}) copy-start(s32[128,8]{0,1:T(8,128)} %param.26) | copy-start | bytes 12292
  133.1 133.9 %all-to-all-start.4 = ((bf16[16,2048,128]{2,1,0:T(8,128)(2,1)}), bf16[16,2048,128]{2,1,0:T(8,128)(2,1)}, u32[]{:S(2)}, u32[]{:S(2)}) async-start(bf16[16,2048,128]{2,1,0:T(8,128)(2,1)} %stack.3), calls=%async_computation.4 | async-start | bytes 16777216 | tf_op jit(solution)/shard_map/all_to_all | solution.py:18
  141.9 125.1 %copy-start.1 = (bf16[128,2048]{1,0:T(8,128)(2,1)S(1)}, bf16[128,2048]{1,0:T(8,128)(2,1)}, u32[]{:S(2)}) copy-start(bf16[128,2048]{1,0:T(8,128)(2,1)} %param.15) | copy-start | bytes 1572868
  145.6 128.5 %copy-start.7 = (f32[2048]{0:T(1024)S(1)}, f32[2048]{0:T(1024)}, u32[]{:S(2)}) copy-start(f32[2048]{0:T(1024)} %param.22) | copy-start | bytes 24580
  273.3 0.8 copy-start.2
  275.6 25.8 %all-to-all-start.5 = ((bf16[16,16,2048]{2,1,0:T(8,128)(2,1)}), bf16[16,16,2048]{2,1,0:T(8,128)(2,1)}, u32[]{:S(2)}, u32[]{:S(2)}) async-start(bf16[16,16,2048]{2,1,0:T(8,128)(2,1)} %bitcast.42), calls=%async_computation.5 | async-start | bytes 2097152 | tf_op jit(solution)/shard_map/all_to_all | solution.py:167
  296.1 15.9 %copy-start.5 = (f32[128,8]{0,1:T(8,128)S(1)}, f32[128,8]{0,1:T(8,128)}, u32[]{:S(2)}) copy-start(f32[128,8]{0,1:T(8,128)} %param.27) | copy-start | bytes 12292
  307.5 20.1 %all-to-all-start.6 = ((bf16[16,16,2048]{2,1,0:T(8,128)(2,1)}), bf16[16,16,2048]{2,1,0:T(8,128)(2,1)S(1)}, u32[]{:S(2)}, u32[]{:S(2)}) async-start(bf16[16,16,2048]{2,1,0:T(8,128)(2,1)} %convolution_convert_fusion), calls=%async_computation.6 | async-start | bytes 2097152 | tf_op jit(solution)/shard_map/all_to_all | solution.py:174
Sparse Core Ops, SparseCore 0:
  17.7 73.7 all-gather.2
